TPU v7x, 256 devices: a whole 4x4x8 slice. The times are simulated.
256 devices in a mesh: ctx: 32 (over z, x), tp: 8 (over y, core).
Axes of the slice: x: 4, y: 4, z: 8, core: 2. Of those that a mesh axis runs over, the one named last changes fastest.
Arguments:
- activations: bfloat16 [8192, 4096], P('ctx'), may hold values from -38 to 38
- w_qkv: bfloat16 [4096, 6144], P(None, 'tp'), may hold values from -0.09375 to 0.09375
- matching: int32 [8, 32], P('tp'), may hold values from 0 to 31, each once within a row
- dropout_bits: int32 [8192, 512], P('ctx', 'tp'), may hold values from 0 to 65535
- out_grad: bfloat16 [8192, 2048], P('ctx', 'tp'), may hold values from -0.29882812 to 0.29882812
Outputs:
- attended: bfloat16 [8192, 2048], P('ctx', 'tp')
- input_grad: bfloat16 [8192, 4096], P('ctx', 'tp')
- weight_grad: bfloat16 [4096, 6144], P('ctx', 'tp')
Inputs may be any that keep to these rules, and one draw needn't show every extreme that they name: Each row of matching is a permutation of the 32 blocks.
All inputs are finite; a program needn't handle non-finite values.
Results may differ from a plain program's by a relative error of at most 0.019.
Values may be sent and summed in bfloat16 or wider, within the bound.
No kernel may reach another device: no remote copies, remote signals or barrier semaphores. Data moves between devices by JAX's collectives and lax.ppermute only.
A program may use at most 128 MiB of HBM per device.

v0:
```python
import jax
import jax.numpy as jnp
import numpy as np
from jax import lax
from jax.sharding import PartitionSpec as P

HD = 128
BLK = 256
HGROUP = 2
WORDS = 32


def unpack_bits(words):
    shifts = jnp.arange(16, dtype=jnp.int32)
    bits = jnp.bitwise_and(jnp.right_shift(words[..., None], shifts), 1)
    return bits.reshape(words.shape[:-1] + (words.shape[-1] * 16,)).astype(jnp.float32) * 2.0


def to_blocks(flat, width):
    row_total = flat.shape[0]
    head_count = flat.shape[1] // width
    return flat.reshape(row_total // BLK, BLK, head_count, width).transpose(2, 0, 1, 3)


def from_blocks(blocked):
    head_count, block_count, block_rows, width = blocked.shape
    return blocked.transpose(1, 2, 0, 3).reshape(block_count * block_rows, head_count * width)


def pick_rows(current, shard_rows, wanted_rows, first_row):
    row_count = shard_rows.shape[0]
    head_count = wanted_rows.shape[0]
    width = shard_rows.shape[1] // head_count
    by_head = shard_rows.reshape(row_count, head_count, width).transpose(1, 0, 2)
    offset = wanted_rows.reshape(head_count, -1) - first_row
    within = (offset >= 0) & (offset < row_count)
    picked = jnp.take_along_axis(by_head, jnp.clip(offset, 0, row_count - 1)[:, :, None], axis=1)
    merged = jnp.where(within[:, :, None], picked, current.reshape(head_count, -1, width))
    return merged.reshape(current.shape)


def per_device(activations, w_qkv, matching, dropout_bits, out_grad):
    f32 = jnp.float32
    local_tokens = activations.shape[0]
    head_count = out_grad.shape[1] // HD
    local_blocks = local_tokens // BLK
    score_scale = HD ** (-0.5)
    ctx_index = lax.axis_index("ctx")
    projected = jnp.dot(activations, w_qkv, preferred_element_type=f32).astype(jnp.bfloat16)
    projected = projected.reshape(local_tokens, head_count, 3, HD)
    query_flat = projected[:, :, 0].reshape(local_tokens, head_count * HD)
    key_flat = projected[:, :, 1].reshape(local_tokens, head_count * HD)
    value_flat = projected[:, :, 2].reshape(local_tokens, head_count * HD)
    query = to_blocks(query_flat, HD)
    key_own = to_blocks(key_flat, HD)
    value_own = to_blocks(value_flat, HD)
    head_match = matching[np.arange(head_count) // HGROUP]
    all_blocks = head_match.shape[1]
    matched = lax.dynamic_slice_in_dim(head_match, ctx_index * local_blocks, local_blocks, 1)
    in_block = jnp.arange(BLK, dtype=jnp.int32)
    key_rows = matched[:, :, None] * BLK + in_block
    empty_rows = jnp.zeros((head_count, local_blocks, BLK, HD), jnp.bfloat16)
    first_row = jnp.int32(0)
    key_far = pick_rows(
        empty_rows, lax.all_gather(key_flat, "ctx", axis=0, tiled=True), key_rows, first_row
    )
    value_far = pick_rows(
        empty_rows, lax.all_gather(value_flat, "ctx", axis=0, tiled=True), key_rows, first_row
    )
    keys = jnp.concatenate([key_own, key_far], 2)
    values = jnp.concatenate([value_own, value_far], 2)
    scores = jnp.einsum("hnqd,hnkd->hnqk", query, keys, preferred_element_type=f32) * score_scale
    row_max = jnp.max(scores, -1, keepdims=True)
    log_total = row_max + jnp.log(jnp.sum(jnp.exp(scores - row_max), -1, keepdims=True))
    probability = jnp.exp(scores - log_total)
    kept = unpack_bits(to_blocks(dropout_bits, WORDS))
    dropped = (probability * kept).astype(jnp.bfloat16)
    attended = jnp.einsum("hnqk,hnkd->hnqd", dropped, values, preferred_element_type=f32).astype(
        jnp.bfloat16
    )
    grad_out = to_blocks(out_grad, HD)
    grad_prob = jnp.einsum("hnqd,hnkd->hnqk", grad_out, values, preferred_element_type=f32) * kept
    row_delta = jnp.sum(probability * grad_prob, -1, keepdims=True)
    grad_score = (probability * (grad_prob - row_delta) * score_scale).astype(jnp.bfloat16)
    grad_query = jnp.einsum("hnqk,hnkd->hnqd", grad_score, keys, preferred_element_type=f32).astype(
        jnp.bfloat16
    )
    grad_keys = jnp.einsum("hnqk,hnqd->hnkd", grad_score, query, preferred_element_type=f32)
    grad_values = jnp.einsum("hnqk,hnqd->hnkd", dropped, grad_out, preferred_element_type=f32)
    inverse = (
        jnp.zeros_like(head_match)
        .at[np.arange(head_count)[:, None], head_match]
        .set(jnp.broadcast_to(jnp.arange(all_blocks, dtype=jnp.int32)[None, :], head_match.shape))
    )
    sources = lax.dynamic_slice_in_dim(inverse, ctx_index * local_blocks, local_blocks, 1)
    query_rows = sources[:, :, None] * BLK + in_block
    far_part = jnp.concatenate([grad_keys[:, :, BLK:], grad_values[:, :, BLK:]], -1).astype(
        jnp.bfloat16
    )
    far_flat = from_blocks(far_part)
    empty_terms = jnp.zeros((head_count, local_blocks, BLK, 2 * HD), jnp.bfloat16)
    returned = pick_rows(
        empty_terms, lax.all_gather(far_flat, "ctx", axis=0, tiled=True), query_rows, jnp.int32(0)
    )
    far_key = returned[..., :HD].astype(f32)
    far_value = returned[..., HD:].astype(f32)
    grad_key = (grad_keys[:, :, :BLK] + far_key).astype(jnp.bfloat16)
    grad_value = (grad_values[:, :, :BLK] + far_value).astype(jnp.bfloat16)
    stacked = jnp.stack([grad_query, grad_key, grad_value], 3)
    grad_qkv = stacked.transpose(1, 2, 0, 3, 4).reshape(local_tokens, head_count * 3 * HD)
    weight_grad = lax.psum_scatter(
        lax.dot_general(
            activations, grad_qkv, (((0,), (0,)), ((), ())), preferred_element_type=f32
        ).astype(jnp.bfloat16),
        "ctx",
        scatter_dimension=0,
        tiled=True,
    )
    input_grad = lax.psum_scatter(
        lax.dot_general(w_qkv, grad_qkv, (((1,), (1,)), ((), ())), preferred_element_type=f32),
        "tp",
        scatter_dimension=0,
        tiled=True,
    ).T.astype(jnp.bfloat16)
    return (from_blocks(attended), input_grad, weight_grad)


def solution(mesh):
    return jax.shard_map(
        per_device,
        mesh=mesh,
        in_specs=(P("ctx", None), P(None, "tp"), P("tp", None), P("ctx", "tp"), P("ctx", "tp")),
        out_specs=(P("ctx", "tp"), P("ctx", "tp"), P("ctx", "tp")),
        check_vma=False,
    )
```

profile of v0, /device:TPU:8, one launch (start us, length us, event | category | flops | bytes accessed | tf_op | source)
XLA Modules:
  0.0 628.6 jit_solution(16482032936210440719)
XLA Ops:
  7.3 1.5 copy-done
  8.8 4.6 convolution_convert_fusion.1
  13.3 0.2 copy.44
  13.5 0.7 fusion.41
  14.3 0.7 all-gather.6.cloned.1.call-update
  15.1 1.0 copy.74
  16.1 1.7 copy.73
  17.8 0.6 fusion.42
  18.4 0.6 or_bitcast_fusion
  19.2 0.8 copy.72
  20.1 1.4 copy.49
  21.5 0.6 and_bitcast_fusion
  22.1 0.6 compare_and_fusion.2
  22.7 77.1 %all-gather.4.cloned.1.call-done = bf16[8192,256]{0,1:T(8,128)(2,1)} async-done(((bf16[256,256]{0,1:T(8,128)(2,1)}), bf16[8192,256]{0,1:T(8,128)(2,1)}) %all-gather.4.cloned.1.call-update) | async-done | bytes 4194320 | tf_op jit(solution)/shard_map/all_gather | solution.py:65
  99.9 6.3 %copy.48 = bf16[8192,2,128]{2,0,1:T(8,128)(2,1)} copy(bf16[8192,2,128]{0,2,1:T(8,128)(2,1)} %bitcast.125) | data formatting | bytes 8388608 | tf_op jit(solution)/shard_map/reshape | solution.py:34
  106.2 80.0 %all-gather.6.cloned.1.call-done = bf16[8192,256]{0,1:T(8,128)(2,1)} async-done(((bf16[256,256]{0,1:T(8,128)(2,1)}), bf16[8192,256]{0,1:T(8,128)(2,1)}) %all-gather.6.cloned.1.call-update) | async-done | bytes 4194320 | tf_op jit(solution)/shard_map/all_gather | solution.py:68
  186.2 6.4 %copy.52 = bf16[8192,2,128]{2,0,1:T(8,128)(2,1)} copy(bf16[8192,2,128]{0,2,1:T(8,128)(2,1)} %bitcast.126) | data formatting | bytes 8388608 | tf_op jit(solution)/shard_map/reshape | solution.py:34
  192.6 6.7 %gather_fusion.1 = bf16[512,128]{1,0:T(8,128)(2,1)S(1)} fusion(bf16[2,8192,128]{2,1,0:T(8,128)(2,1)} %bitcast.123, s32[512]{0:T(512)S(1)} %bitcast.118), kind=kCustom, calls=%fused_computation.clone | custom fusion | bytes 266240 | tf_op jit(solution)/shard_map/jit(take_along_axis)/gather | solution.py:37
  199.3 6.7 %gather_fusion.2 = bf16[512,128]{1,0:T(8,128)(2,1)S(1)} fusion(bf16[2,8192,128]{2,1,0:T(8,128)(2,1)} %bitcast.124, s32[512]{0:T(512)S(1)} %bitcast.119), kind=kCustom, calls=%fused_computation.1.clone | custom fusion | bytes 266240 | tf_op jit(solution)/shard_map/jit(take_along_axis)/gather | solution.py:37
  206.0 0.2 fusion.25
  206.2 0.6 copy-done.4
  206.9 1.3 fusion.43
  208.2 0.3 exponential_reduce_fusion
  208.6 1.5 multiply_convert_fusion
  210.1 0.8 copy-done.1
  210.9 1.0 convolution_bitcast_fusion.2
  211.9 2.6 fusion.5
  214.5 5.2 convolution_bitcast_fusion.3
  219.7 1.0 slice.70
  220.7 1.0 slice.69
  221.7 0.7 pad_maximum_fusion
  222.4 0.2 reduce-scatter.5.cloned.1.call-start
  222.9 3.5 scatter_fusion
  226.3 0.2 multiply_reduce_fusion.1
  226.7 4.6 fusion.7
  231.3 94.2 %all-gather.8.cloned.1.call-done = bf16[8192,512]{0,1:T(8,128)(2,1)} async-done(((bf16[256,512]{0,1:T(8,128)(2,1)}), bf16[8192,512]{0,1:T(8,128)(2,1)}) %all-gather.8.cloned.1.call-update) | async-done | bytes 8388624 | tf_op jit(solution)/shard_map/all_gather | solution.py:103
  325.5 12.0 %copy.59 = bf16[8192,2,256]{2,0,1:T(8,128)(2,1)} copy(bf16[8192,2,256]{0,2,1:T(8,128)(2,1)} %bitcast.122) | data formatting | bytes 16777216 | tf_op jit(solution)/shard_map/reshape | solution.py:34
  337.5 6.9 %gather_fusion = bf16[512,256]{1,0:T(8,128)(2,1)S(1)} fusion(bf16[2,8192,256]{2,1,0:T(8,128)(2,1)} %bitcast.121, s32[512]{0:T(512)S(1)} %bitcast.120), kind=kCustom, calls=%fused_computation.2 | custom fusion | bytes 528384 | tf_op jit(solution)/shard_map/jit(take_along_axis)/gather | solution.py:37
  344.6 1.0 fusion.21
  345.7 6.6 %convolution_bitcast_fusion = f32[4096,256]{0,1:T(8,128)} fusion(bf16[256,768]{0,1:T(8,128)(2,1)S(1)} %bitcast.128, bf16[4096,768]{1,0:T(8,128)(2,1)} %param.12), kind=kOutput, calls=%fused_computation.7 | convolution fusion | flops 1610612736 | bytes 10878976 | tf_op jit(solution)/shard_map/dot_general | solution.py:120
  352.3 4.5 fusion.1
  356.8 8.6 %copy.70 = bf16[4096,768]{1,0:T(8,128)(2,1)} copy(bf16[4096,768]{0,1:T(8,128)(2,1)} %fusion.1) | data formatting | bytes 12582912
  365.5 1.0 copy-done.2
  366.5 0.3 convolution_convert_fusion.3
  366.8 0.8 copy.62
  367.6 20.7 %reduce-scatter.5.cloned.1.call-done = f32[512,256]{0,1:T(8,128)} async-done(((f32[4096,256]{0,1:T(8,128)}), f32[512,256]{0,1:T(8,128)}) %reduce-scatter.5.cloned.1.call-update) | async-done | bytes 524304 | tf_op jit(solution)/shard_map/reduce_scatter | solution.py:119
  388.3 1.8 convert_bitcast_fusion
  390.0 232.0 %reduce-scatter.7.cloned.1.call-done = bf16[128,768]{1,0:T(8,128)(2,1)} async-done(((bf16[4096,768]{1,0:T(8,128)(2,1)}), bf16[128,768]{1,0:T(8,128)(2,1)}) %reduce-scatter.7.cloned.1.call-update) | async-done | bytes 196624
  (40 shorter events, 1.1 us)
Async XLA Ops:
  7.2 1.6 copy-start
  7.2 10.6 %copy-start.7 = (s32[1,32]{1,0:T(1,128)S(1)}, s32[1,32]{1,0:T(1,128)}, u32[]{:S(2)}) copy-start(s32[1,32]{1,0:T(1,128)} %param.13) | copy-start | bytes 388
  7.2 11.9 %copy-start.5 = (bf16[256,256]{1,0:T(8,128)(2,1)S(1)}, bf16[256,256]{1,0:T(8,128)(2,1)}, u32[]{:S(2)}) copy-start(bf16[256,256]{1,0:T(8,128)(2,1)} %param.15) | copy-start | bytes 393220
  7.2 12.8 %copy-start.6 = (s32[256,64]{0,1:T(8,128)S(1)}, s32[256,64]{0,1:T(8,128)}, u32[]{:S(2)}) copy-start(s32[256,64]{0,1:T(8,128)} %param.14) | copy-start | bytes 196612
  7.2 92.7 %all-gather.4.cloned.1.call-start = ((), (), s32[]{:S(2)}) async-start(), calls=%async_computation.2 | async-start | bytes 4325376 | tf_op jit(solution)/shard_map/all_gather | solution.py:65
  14.3 172.0 %all-gather.6.cloned.1.call-start = ((), (), s32[]{:S(2)}) async-start(), calls=%async_computation.3 | async-start | bytes 4325376 | tf_op jit(solution)/shard_map/all_gather | solution.py:68
  15.0 310.5 %all-gather.8.cloned.1.call-start = ((), (), s32[]{:S(2)}) async-start(), calls=%async_computation.4 | async-start | bytes 8650752 | tf_op jit(solution)/shard_map/all_gather | solution.py:103
  206.2 0.7 copy-start.4
  210.1 0.8 copy-start.1
  222.4 165.8 %reduce-scatter.5.cloned.1.call-start = ((), (), s32[]{:S(2)}) async-start(), calls=%async_computation.5 | async-start | bytes 4718592 | tf_op jit(solution)/shard_map/reduce_scatter | solution.py:119
  325.5 19.1 %copy-start.3 = (f32[2,1,512,128]{2,3,0,1:T(8,128)S(1)}, f32[2,1,512,128]{2,3,0,1:T(8,128)}, u32[]{:S(2)}) copy-start(f32[2,1,512,128]{2,3,0,1:T(8,128)} %convolution_bitcast_fusion.2) | copy-start | bytes 1572868
  352.3 269.8 %reduce-scatter.7.cloned.1.call-start = ((), (), s32[]{:S(2)}) async-start(), calls=%async_computation.6 | async-start | bytes 6488064
  365.4 1.1 copy-start.2
Sparse Core Ops, SparseCore 0:
  14.4 85.4 all-gather.3
  102.9 83.2 all-gather.5
  222.6 102.8 all-gather.7
  352.4 35.8 reduce-scatter.4
  392.7 229.3 reduce-scatter.6
where the time goes:
time: 630 us; the launch traced here: 629 us
  waiting for transfers between devices  505 us (80%)
  local copies, waits for them, and re-layouts  70.1 us (11%)
  matrix products  30.7 us (5%)
  between operations  14 us (2%)
  other arithmetic  8.57 us (1%)
    unnamed x6, waiting for transfers between devices  233 us
    all_gather x1, waiting for transfers between devices, per_device(): lax.all_gather(far_flat, 'ctx', axis=0, tiled=True)  94.2 us
    all_gather x1, waiting for transfers between devices, per_device(): lax.all_gather(value_flat, 'ctx', axis=0, tiled=True)  80 us
    all_gather x1, waiting for transfers between devices, per_device(): lax.all_gather(key_flat, 'ctx', axis=0, tiled=True)  77.1 us
    reshape x3, local copies, waits for them, and re-layouts, pick_rows(): shard_rows.reshape(row_count, head_count, width).transpose(1, 0, 2)  24.7 us
    reduce_scatter x1, waiting for transfers between devices, per_device(): lax.psum_scatter(lax.dot_general(w_qkv, grad_qkv, (((1,), (1,)), ((), ())...  20.7 us
    gather x4, local copies, waits for them, and re-layouts, pick_rows(): jnp.take_along_axis(by_head, jnp.clip(offset, 0, row_count - 1)[:, :, Non...  20.4 us
    unnamed x23, local copies, waits for them, and re-layouts  16.8 us
  transfers between devices with their start and end apart: 5, of which 5 were waited for; matrix products, arithmetic and copies ran while one was open for 6% of the time, Pallas kernels for 0%

commit v1 on v0

--- a/solution.py
+++ b/solution.py
@@ -61,9 +61,11 @@
     key_rows = matched[:, :, None] * BLK + in_block
     empty_rows = jnp.zeros((head_count, local_blocks, BLK, HD), jnp.bfloat16)
     first_row = jnp.int32(0)
-    key_far = pick_rows(
-        empty_rows, lax.all_gather(key_flat, "ctx", axis=0, tiled=True), key_rows, first_row
+    prepare_cycles = lambda xx: jnp.concatenate(
+        lax.all_to_all(jnp.stack([xx for _ in range(lax.axis_size("ctx"))], axis=0), "ctx", 0, 0),
+        axis=0,
     )
+    key_far = pick_rows(empty_rows, prepare_cycles(key_flat), key_rows, first_row)
     value_far = pick_rows(
         empty_rows, lax.all_gather(value_flat, "ctx", axis=0, tiled=True), key_rows, first_row
     )

time: 630 us -> 616 us (0.978)
  waiting for transfers between devices: 505 us -> 463 us
  local copies, waits for them, and re-layouts: 70.1 us -> 85.3 us
  starting transfers between devices: 0.38 us -> 11.9 us
    all_gather x1 -> x0, waiting for transfers between devices: 77.1 us -> none  [per_device(): lax.all_gather(key_flat, 'ctx', axis=0, tiled=True)]
    all_gather x1, waiting for transfers between devices: 80 us -> 118 us  [per_device(): lax.all_gather(value_flat, 'ctx', axis=0, tiled=True)]
    another operation x1 -> x4, local copies, waits for them, and re-layouts: 0.01 us -> 16.1 us  [the longest x2 13.7 us: pick_rows(): shard_rows.reshape(row_count, head_count, width).transpose(1, 0, 2)]
    all_to_all x0 -> x1, starting transfers between devices: none -> 11.6 us  [per_device(): lax.all_to_all(jnp.stack([xx for _ in range(lax.axis_size('ctx'))], axis=...]
    all_to_all x0 -> x1, local copies, waits for them, and re-layouts: none -> 6.5 us  [per_device(): lax.all_to_all(jnp.stack([xx for _ in range(lax.axis_size('ctx'))], axis=...]
    reshape x3 -> x2, local copies, waits for them, and re-layouts: 24.7 us -> 18.3 us  [pick_rows(): shard_rows.reshape(row_count, head_count, width).transpose(1, 0, 2)]
    unnamed x6 -> x5, waiting for transfers between devices: 233 us -> 232 us
  transfers between devices with their start and end apart: 5 -> 5, of which waited for: 5 -> 4; matrix products, arithmetic and copies ran while one was open for 6% -> 6% of each run, Pallas kernels for 0% -> 0%
where the time goes in v1:
time: 616 us; the launch traced here: 614 us
  waiting for transfers between devices  463 us (75%)
  local copies, waits for them, and re-layouts  85.3 us (14%)
  matrix products  30.8 us (5%)
  between operations  14 us (2%)
  starting transfers between devices  11.9 us (2%)
  other arithmetic  8.54 us (1%)
    unnamed x5, waiting for transfers between devices  232 us
    all_gather x1, waiting for transfers between devices, per_device(): lax.all_gather(value_flat, 'ctx', axis=0, tiled=True)  118 us
    all_gather x1, waiting for transfers between devices, per_device(): lax.all_gather(far_flat, 'ctx', axis=0, tiled=True)  92.7 us
    reduce_scatter x1, waiting for transfers between devices, per_device(): lax.psum_scatter(lax.dot_general(w_qkv, grad_qkv, (((1,), (1,)), ((), ())...  20.7 us
    gather x4, local copies, waits for them, and re-layouts, pick_rows(): jnp.take_along_axis(by_head, jnp.clip(offset, 0, row_count - 1)[:, :, Non...  20.4 us
    reshape x2, local copies, waits for them, and re-layouts, pick_rows(): shard_rows.reshape(row_count, head_count, width).transpose(1, 0, 2)  18.3 us
    unnamed x23, local copies, waits for them, and re-layouts  15.1 us
    another operation x2, local copies, waits for them, and re-layouts, pick_rows(): shard_rows.reshape(row_count, head_count, width).transpose(1, 0, 2)  13.7 us
  transfers between devices with their start and end apart: 5, of which 4 were waited for; matrix products, arithmetic and copies ran while one was open for 6% of the time, Pallas kernels for 0%

profile of v1, /device:TPU:8, one launch (start us, length us, event | category | flops | bytes accessed | tf_op | source)
XLA Modules:
  0.0 614.0 jit_solution(260116843082278978)
XLA Ops:
  7.2 1.5 copy-done
  8.8 4.6 convolution_convert_fusion.1
  13.5 0.7 fusion.41
  14.2 2.4 stack.15
  16.6 11.6 %all-to-all-start = ((bf16[32,256,256]{1,2,0:T(8,128)(2,1)}), bf16[32,256,256]{1,2,0:T(8,128)(2,1)}, u32[]{:S(2)}, u32[]{:S(2)}) async-start(bf16[32,256,256]{1,2,0:T(8,128)(2,1)} %stack.15), calls=%async_computation | async-start | bytes 8388608 | tf_op jit(solution)/shard_map/all_to_all | solution.py:65
  28.4 0.8 copy.74
  29.2 0.6 fusion.42
  29.8 0.6 or_bitcast_fusion
  30.6 0.8 copy.73
  31.4 0.9 shift_right_arithmetic.25
  32.3 1.3 copy.50
  33.6 0.6 and_bitcast_fusion
  34.2 0.6 compare_and_fusion.2
  34.9 117.9 %all-gather.3.cloned.1.call-done = bf16[8192,256]{0,1:T(8,128)(2,1)} async-done(((bf16[256,256]{0,1:T(8,128)(2,1)}), bf16[8192,256]{0,1:T(8,128)(2,1)}) %all-gather.3.cloned.1.call-update) | async-done | bytes 4194320 | tf_op jit(solution)/shard_map/all_gather | solution.py:70
  152.7 6.3 %copy.53 = bf16[8192,2,128]{2,0,1:T(8,128)(2,1)} copy(bf16[8192,2,128]{0,2,1:T(8,128)(2,1)} %bitcast.126) | data formatting | bytes 8388608 | tf_op jit(solution)/shard_map/reshape | solution.py:34
  159.0 6.5 %copy.48 = bf16[32,256,256]{1,0,2:T(8,128)(2,1)} copy(bf16[32,256,256]{1,2,0:T(8,128)(2,1)} %all-to-all-done) | data formatting | bytes 8388608 | tf_op jit(solution)/shard_map/all_to_all | solution.py:65
  165.5 7.4 %reshape_reshape.3 = bf16[8192,2,128]{0,2,1:T(8,128)(2,1)} reshape(bf16[32,256,256]{1,0,2:T(8,128)(2,1)} %copy.48) | data formatting | bytes 8388608 | tf_op jit(solution)/shard_map/reshape;reshape | solution.py:34
  173.0 6.3 %copy.49 = bf16[8192,2,128]{2,0,1:T(8,128)(2,1)} copy(bf16[8192,2,128]{0,2,1:T(8,128)(2,1)} %reshape_reshape.3) | data formatting | bytes 8388608 | tf_op jit(solution)/shard_map/reshape;reshape | solution.py:34
  179.3 6.7 %gather_fusion.2 = bf16[512,128]{1,0:T(8,128)(2,1)S(1)} fusion(bf16[2,8192,128]{2,1,0:T(8,128)(2,1)} %bitcast.124, s32[512]{0:T(512)S(1)} %bitcast.119), kind=kCustom, calls=%fused_computation.1.clone | custom fusion | bytes 266240 | tf_op jit(solution)/shard_map/jit(take_along_axis)/gather | solution.py:37
  185.9 6.8 %gather_fusion.1 = bf16[512,128]{1,0:T(8,128)(2,1)S(1)} fusion(bf16[2,8192,128]{2,1,0:T(8,128)(2,1)} %bitcast.125, s32[512]{0:T(512)S(1)} %bitcast.120), kind=kCustom, calls=%fused_computation.clone | custom fusion | bytes 266240 | tf_op jit(solution)/shard_map/jit(take_along_axis)/gather | solution.py:37
  192.7 0.2 fusion.25
  192.9 0.6 copy-done.5
  193.6 1.4 fusion.43
  194.9 0.3 exponential_reduce_fusion
  195.2 1.6 multiply_convert_fusion
  196.8 0.8 copy-done.1
  197.6 1.0 convolution_bitcast_fusion.2
  198.6 2.5 fusion.5
  201.2 5.3 convolution_bitcast_fusion.3
  206.5 1.0 slice.70
  207.5 1.0 slice.69
  208.4 0.7 pad_maximum_fusion
  209.2 0.2 reduce-scatter.5.cloned.1.call-start
  209.6 3.5 scatter_fusion
  213.5 4.7 fusion.7
  218.1 92.7 %all-gather.5.cloned.1.call-done = bf16[8192,512]{0,1:T(8,128)(2,1)} async-done(((bf16[256,512]{0,1:T(8,128)(2,1)}), bf16[8192,512]{0,1:T(8,128)(2,1)}) %all-gather.5.cloned.1.call-update) | async-done | bytes 8388624 | tf_op jit(solution)/shard_map/all_gather | solution.py:105
  310.9 12.0 %copy.60 = bf16[8192,2,256]{2,0,1:T(8,128)(2,1)} copy(bf16[8192,2,256]{0,2,1:T(8,128)(2,1)} %bitcast.123) | data formatting | bytes 16777216 | tf_op jit(solution)/shard_map/reshape | solution.py:34
  322.9 6.8 %gather_fusion = bf16[512,256]{1,0:T(8,128)(2,1)S(1)} fusion(bf16[2,8192,256]{2,1,0:T(8,128)(2,1)} %bitcast.122, s32[512]{0:T(512)S(1)} %bitcast.121), kind=kCustom, calls=%fused_computation.2 | custom fusion | bytes 528384 | tf_op jit(solution)/shard_map/jit(take_along_axis)/gather | solution.py:37
  329.9 1.0 fusion.21
  331.0 6.6 %convolution_bitcast_fusion = f32[4096,256]{0,1:T(8,128)} fusion(bf16[256,768]{0,1:T(8,128)(2,1)S(1)} %bitcast.128, bf16[4096,768]{1,0:T(8,128)(2,1)} %param.12), kind=kOutput, calls=%fused_computation.7 | convolution fusion | flops 1610612736 | bytes 10878976 | tf_op jit(solution)/shard_map/dot_general | solution.py:122
  337.7 4.5 fusion.1
  342.1 8.7 %copy.71 = bf16[4096,768]{1,0:T(8,128)(2,1)} copy(bf16[4096,768]{0,1:T(8,128)(2,1)} %fusion.1) | data formatting | bytes 12582912
  350.8 1.0 copy-done.2
  351.8 0.3 convolution_convert_fusion.3
  352.2 0.8 copy.63
  352.9 20.7 %reduce-scatter.5.cloned.1.call-done = f32[512,256]{0,1:T(8,128)} async-done(((f32[4096,256]{0,1:T(8,128)}), f32[512,256]{0,1:T(8,128)}) %reduce-scatter.5.cloned.1.call-update) | async-done | bytes 524304 | tf_op jit(solution)/shard_map/reduce_scatter | solution.py:121
  373.6 1.8 convert_bitcast_fusion
  375.4 232.1 %reduce-scatter.7.cloned.1.call-done = bf16[128,768]{1,0:T(8,128)(2,1)} async-done(((bf16[4096,768]{1,0:T(8,128)(2,1)}), bf16[128,768]{1,0:T(8,128)(2,1)}) %reduce-scatter.7.cloned.1.call-update) | async-done | bytes 196624
  (42 shorter events, 1.5 us)
Async XLA Ops:
  7.2 1.6 copy-start
  7.2 145.5 %all-gather.3.cloned.1.call-start = ((), (), s32[]{:S(2)}) async-start(), calls=%async_computation.3 | async-start | bytes 4325376 | tf_op jit(solution)/shard_map/all_gather | solution.py:70
  16.6 11.6 %copy-start.4 = (bf16[256,2,1,128]{0,3,2,1:T(8,128)(2,1)S(1)}, bf16[256,2,1,128]{0,3,2,1:T(8,128)(2,1)}, u32[]{:S(2)}) copy-start(bf16[256,2,1,128]{0,3,2,1:T(8,128)(2,1)} %get-tuple-element.13) | copy-start | bytes 393220
  16.6 12.5 %copy-start.7 = (s32[1,32]{1,0:T(1,128)S(1)}, s32[1,32]{1,0:T(1,128)}, u32[]{:S(2)}) copy-start(s32[1,32]{1,0:T(1,128)} %param.13) | copy-start | bytes 388
  16.6 13.9 %copy-start.6 = (bf16[256,256]{1,0:T(8,128)(2,1)S(1)}, bf16[256,256]{1,0:T(8,128)(2,1)}, u32[]{:S(2)}) copy-start(bf16[256,256]{1,0:T(8,128)(2,1)} %param.15) | copy-start | bytes 393220
  16.6 142.4 %all-to-all-start = ((bf16[32,256,256]{1,2,0:T(8,128)(2,1)}), bf16[32,256,256]{1,2,0:T(8,128)(2,1)}, u32[]{:S(2)}, u32[]{:S(2)}) async-start(bf16[32,256,256]{1,2,0:T(8,128)(2,1)} %stack.15), calls=%async_computation | async-start | bytes 8388608 | tf_op jit(solution)/shard_map/all_to_all | solution.py:65
  28.2 282.6 %all-gather.5.cloned.1.call-start = ((), (), s32[]{:S(2)}) async-start(), calls=%async_computation.4 | async-start | bytes 8650752 | tf_op jit(solution)/shard_map/all_gather | solution.py:105
  192.9 0.7 copy-start.5
  196.8 0.8 copy-start.1
  209.2 164.4 %reduce-scatter.5.cloned.1.call-start = ((), (), s32[]{:S(2)}) async-start(), calls=%async_computation.5 | async-start | bytes 4718592 | tf_op jit(solution)/shard_map/reduce_scatter | solution.py:121
  310.9 19.0 %copy-start.3 = (f32[2,1,512,128]{2,3,0,1:T(8,128)S(1)}, f32[2,1,512,128]{2,3,0,1:T(8,128)}, u32[]{:S(2)}) copy-start(f32[2,1,512,128]{2,3,0,1:T(8,128)} %convolution_bitcast_fusion.2) | copy-start | bytes 1572868
  337.6 269.8 %reduce-scatter.7.cloned.1.call-start = ((), (), s32[]{:S(2)}) async-start(), calls=%async_computation.6 | async-start | bytes 6488064
  350.8 1.1 copy-start.2
Sparse Core Ops, SparseCore 0:
  14.3 138.3 all-gather.2
  209.3 101.5 all-gather.4
  337.7 35.8 reduce-scatter.4
  378.0 229.3 reduce-scatter.6
